TPU v7x, 512 devices: a whole 4x8x8 slice. The times are simulated.
512 devices in a mesh: dp: 16 (over y, core), ctx: 32 (over z, x).
Axes of the slice: x: 4, y: 8, z: 8, core: 2. Of those that a mesh axis runs over, the one named last changes fastest.
Arguments:
- inner_gate: bfloat16 [65536, 1024], P(('dp', 'ctx')), parts along dimension 0, may hold values from -6 to 6
- outer_gate: bfloat16 [65536, 1024], P(('dp', 'ctx')), parts along dimension 0, may hold values from -6 to 6
- signal: bfloat16 [65536, 1024], P(('dp', 'ctx')), parts along dimension 0, may hold values from -6 to 6
- filters: float32 [64, 128], replicated, may hold values from -0.5 to 0.5
- bypass: float32 [1024], replicated, may hold values from 0.5 to 1.5
- query_rows: bfloat16 [65536, 1024], P(('dp', 'ctx')), parts along dimension 0, may hold values from -25 to 25
- key_rows: bfloat16 [65536, 1024], P(('dp', 'ctx')), parts along dimension 0, may hold values from -4.5 to 4.5
Outputs:
- hyena_out: bfloat16 [65536, 1024], P(('dp', 'ctx')), parts along dimension 0
- attended: bfloat16 [65536, 1024], P(('dp', 'ctx')), parts along dimension 0
There are 16 independent parts, one for each index of `dp`. A program takes and returns all parts, laid end to end along the dimension named above; an argument that names none is the same for every part. Nothing has to cross between parts.
All inputs are finite; a program needn't handle non-finite values.
Results may differ from a plain program's by a relative error of at most 0.006.
Values may be sent and summed in bfloat16 or wider, within the bound.
No kernel may reach another device: no remote copies, remote signals or barrier semaphores. Data moves between devices by JAX's collectives and lax.ppermute only.
A program may use at most 128 MiB of HBM per device.

v0:
```python
import math
import jax
import jax.numpy as jnp
from jax import lax
from jax.sharding import PartitionSpec as P

DH = 128
TAPS = 128


def passed_along(array, axis, by):
    devices = lax.axis_size(axis)
    return lax.ppermute(array, axis, [(i, (i + by) % devices) for i in range(devices)])


def passed_along_2(array, axis, by):
    devices = lax.axis_size(axis)
    pairs = [(i, i + by) for i in range(devices) if 0 <= i + by < devices]
    return lax.ppermute(array, axis, pairs)


def attend(queries, query_pos, key_rows, hyena_out):
    local_rows, channels = queries.shape
    head_count = channels // DH
    query_heads = queries.reshape(local_rows, head_count, DH)
    latest = jnp.max(query_pos)
    inv_root = 1.0 / math.sqrt(DH)

    def update_block(current, key_piece, value_piece, start):
        running_max, running_sum, weighted = current
        piece_rows = key_piece.shape[0]
        key_pos = start + jnp.arange(piece_rows, dtype=jnp.int32)
        key_heads = key_piece.reshape(piece_rows, head_count, DH)
        value_heads = value_piece.reshape(piece_rows, head_count, DH)
        scores = (
            jnp.einsum("thd,phd->thp", query_heads, key_heads, preferred_element_type=jnp.float32)
            * inv_root
        )
        visible = key_pos[None, None, :] <= query_pos[:, None, None]
        scores = jnp.where(visible, scores, -1e30)
        new_max = jnp.maximum(running_max, jnp.max(scores, axis=2))
        weights = jnp.where(visible, jnp.exp(scores - new_max[:, :, None]), 0.0)
        rescale = jnp.exp(running_max - new_max)
        running_sum = running_sum * rescale + jnp.sum(weights, axis=2)
        weighted = weighted * rescale[:, :, None] + jnp.einsum(
            "thp,phd->thd",
            weights.astype(jnp.bfloat16),
            value_heads,
            preferred_element_type=jnp.float32,
        )
        return (new_max, running_sum, weighted)

    def guarded(current, key_piece, value_piece, start):

        def unchanged(state):
            return state

        def changed(state):
            return update_block(state, key_piece, value_piece, start)

        return lax.cond(start > latest, unchanged, changed, current)

    def fold(softmax_state, pieces, start):
        key_piece, value_piece = pieces
        piece_rows = key_piece.shape[0]
        return guarded(softmax_state, key_piece, value_piece, start)

    initial = (
        jnp.full((local_rows, head_count), -1e30, jnp.float32),
        jnp.zeros((local_rows, head_count), jnp.float32),
        jnp.zeros((local_rows, head_count, DH), jnp.float32),
    )
    members = lax.axis_size("ctx")
    my_index = lax.axis_index("ctx")
    block_rows = key_rows.shape[0]
    stacked = jnp.stack([key_rows, hyena_out])
    first_state = fold(initial, (key_rows, hyena_out), my_index * block_rows)

    def chain_step(step_index, carried):
        current, held = carried
        held = passed_along(held, "ctx", 1)
        anchor = (my_index - 1 - step_index) % members
        current = fold(current, (held[0], held[1]), anchor * block_rows)
        return (current, held)

    softmax_state, last_held = lax.fori_loop(0, members - 1, chain_step, (first_state, stacked))
    final_max, final_sum, weighted = softmax_state
    return (weighted / final_sum[:, :, None]).reshape(local_rows, channels).astype(jnp.bfloat16)


def shards(inner_gate, outer_gate, signal, filters, bypass, query_rows, key_rows):
    local_rows, channels = signal.shape
    members = lax.axis_size("ctx")
    my_index = lax.axis_index("ctx")
    product = (inner_gate.astype(jnp.float32) * signal.astype(jnp.float32)).astype(jnp.bfloat16)
    left_rim = passed_along_2(product[local_rows - (TAPS - 1) :], "ctx", 1)
    extended = jnp.concatenate([left_rim, product], axis=0).astype(jnp.float32)
    group_count = filters.shape[0]
    group_width = channels // group_count
    window_rows = 2 * TAPS - 1
    flipped = filters[:, ::-1]
    padded = jnp.concatenate([flipped, jnp.zeros((group_count, TAPS), jnp.float32)], axis=1)
    banded = jnp.tile(padded, (1, TAPS))[:, : TAPS * window_rows].reshape(
        group_count, TAPS, window_rows
    )
    block_count = local_rows // TAPS
    windows = jnp.stack([extended])
    windows = windows.reshape(block_count, window_rows, group_count, group_width)
    convolved = jnp.einsum(
        "gtj,bjgc->btgc", banded, windows, precision=lax.Precision.HIGHEST
    ).reshape(local_rows, channels)
    hyena_out = (
        outer_gate.astype(jnp.float32) * (convolved + bypass[None, :] * product.astype(jnp.float32))
    ).astype(jnp.bfloat16)
    per_source = local_rows // members
    spread = lax.all_to_all(
        query_rows.reshape(per_source, members, channels),
        "ctx",
        split_axis=1,
        concat_axis=1,
        tiled=True,
    )
    source = jnp.arange(members, dtype=jnp.int32)[None, :]
    offset = jnp.arange(per_source, dtype=jnp.int32)[:, None]
    query_pos = (source * local_rows + offset * members + my_index).reshape(local_rows)
    local_queries = spread.reshape(local_rows, channels)
    attended = attend(local_queries, query_pos, key_rows, hyena_out)
    returned = lax.all_to_all(
        attended.reshape(per_source, members, channels),
        "ctx",
        split_axis=1,
        concat_axis=1,
        tiled=True,
    )
    attended = returned.reshape(local_rows, channels)
    return (hyena_out, attended)


def solution(mesh):
    placed = (
        P(("dp", "ctx"), None),
        P(("dp", "ctx"), None),
        P(("dp", "ctx"), None),
        P(),
        P(),
        P(("dp", "ctx"), None),
        P(("dp", "ctx"), None),
    )
    return jax.shard_map(
        shards,
        mesh=mesh,
        in_specs=placed,
        out_specs=(P(("dp", "ctx"), None), P(("dp", "ctx"), None)),
        check_vma=False,
    )
```

profile of v0, /device:TPU:56, one launch (start us, length us, event | category | flops | bytes accessed | tf_op | source)
XLA Modules:
  0.0 632.5 jit_solution(6121067167949745488)
XLA Ops:
  1.8 3.4 collective-permute-start.1
  7.1 12.9 %all-to-all-start = ((bf16[4,32,1024]{2,0,1:T(4,128)(2,1)}), bf16[4,32,1024]{2,0,1:T(4,128)(2,1)S(1)}, u32[]{:S(2)}, u32[]{:S(2)}) async-start(bf16[4,32,1024]{2,0,1:T(4,128)(2,1)} %copy.49), calls=%async_computation | async-start | bytes 524288 | tf_op jit(solution)/shard_map/all_to_all | solution.py:116
  21.5 4.7 copy.63
  26.2 3.8 slice.27
  30.0 15.9 %reshape.132 = f32[64,128,255]{2,1,0:T(8,128)} reshape(f32[64,32640]{1,0:T(8,128)} %slice.27) | data formatting | bytes 16711680 | tf_op jit(solution)/shard_map/reshape | solution.py:103
  47.6 6.3 fusion.32
  56.4 2.1 conditional.2
  58.6 554.3 %while.22 = (s32[]{:T(128)}, f32[128,8]{0,1:T(8,128)S(1)}, f32[128,8]{0,1:T(8,128)S(1)}, f32[128,8,128]{2,0,1:T(8,128)S(1)}, bf16[2,128,1024]{1,2,0:T(8,128)(2,1...) while((s32[]{:T(128)}, f32[128,8]{0,1:T(8,128)S(1)}, ...), condition=%wide.region_10.11_spmd.clone, body=%wide.region_5.10_spmd.clone.sunk | while | flops 68569488 | bytes 7736928 | solution.py:86
  58.6 3.7 collective-permute-start
  62.9 14.0 %collective-permute-done = bf16[2,128,1024]{1,2,0:T(8,128)(2,1)S(1)} collective-permute-done((bf16[2,128,1024]{1,2,0:T(8,128)(2,1)S(1)}, bf16[2,128,1024]{1,2,0:T(8,128)(2,1)S(1)}, u32[]{:S(2)}, u32[]{:S(2)}) %collective-permute-start) | collective-permute-done | bytes 524320 | tf_op jit(solution)/shard_map/while/body/eval_jaxpr/ppermute | solution.py:13
  78.2 1.9 collective-permute-start
  80.8 14.9 %collective-permute-done = bf16[2,128,1024]{1,2,0:T(8,128)(2,1)S(1)} collective-permute-done((bf16[2,128,1024]{1,2,0:T(8,128)(2,1)S(1)}, bf16[2,128,1024]{1,2,0:T(8,128)(2,1)S(1)}, u32[]{:S(2)}, u32[]{:S(2)}) %collective-permute-start) | collective-permute-done | bytes 524320 | tf_op jit(solution)/shard_map/while/body/eval_jaxpr/ppermute | solution.py:13
  99.5 14.0 %collective-permute-done = bf16[2,128,1024]{1,2,0:T(8,128)(2,1)S(1)} collective-permute-done((bf16[2,128,1024]{1,2,0:T(8,128)(2,1)S(1)}, bf16[2,128,1024]{1,2,0:T(8,128)(2,1)S(1)}, u32[]{:S(2)}, u32[]{:S(2)}) %collective-permute-start) | collective-permute-done | bytes 524320 | tf_op jit(solution)/shard_map/while/body/eval_jaxpr/ppermute | solution.py:13
  114.9 1.9 collective-permute-start
  117.5 13.2 %collective-permute-done = bf16[2,128,1024]{1,2,0:T(8,128)(2,1)S(1)} collective-permute-done((bf16[2,128,1024]{1,2,0:T(8,128)(2,1)S(1)}, bf16[2,128,1024]{1,2,0:T(8,128)(2,1)S(1)}, u32[]{:S(2)}, u32[]{:S(2)}) %collective-permute-start) | collective-permute-done | bytes 524320 | tf_op jit(solution)/shard_map/while/body/eval_jaxpr/ppermute | solution.py:13
  131.9 1.9 collective-permute-start
  134.5 12.3 %collective-permute-done = bf16[2,128,1024]{1,2,0:T(8,128)(2,1)S(1)} collective-permute-done((bf16[2,128,1024]{1,2,0:T(8,128)(2,1)S(1)}, bf16[2,128,1024]{1,2,0:T(8,128)(2,1)S(1)}, u32[]{:S(2)}, u32[]{:S(2)}) %collective-permute-start) | collective-permute-done | bytes 524320 | tf_op jit(solution)/shard_map/while/body/eval_jaxpr/ppermute | solution.py:13
  150.7 11.8 %collective-permute-done = bf16[2,128,1024]{1,2,0:T(8,128)(2,1)S(1)} collective-permute-done((bf16[2,128,1024]{1,2,0:T(8,128)(2,1)S(1)}, bf16[2,128,1024]{1,2,0:T(8,128)(2,1)S(1)}, u32[]{:S(2)}, u32[]{:S(2)}) %collective-permute-start) | collective-permute-done | bytes 524320 | tf_op jit(solution)/shard_map/while/body/eval_jaxpr/ppermute | solution.py:13
  163.8 1.9 collective-permute-start
  166.4 11.8 %collective-permute-done = bf16[2,128,1024]{1,2,0:T(8,128)(2,1)S(1)} collective-permute-done((bf16[2,128,1024]{1,2,0:T(8,128)(2,1)S(1)}, bf16[2,128,1024]{1,2,0:T(8,128)(2,1)S(1)}, u32[]{:S(2)}, u32[]{:S(2)}) %collective-permute-start) | collective-permute-done | bytes 524320 | tf_op jit(solution)/shard_map/while/body/eval_jaxpr/ppermute | solution.py:13
  182.1 11.8 %collective-permute-done = bf16[2,128,1024]{1,2,0:T(8,128)(2,1)S(1)} collective-permute-done((bf16[2,128,1024]{1,2,0:T(8,128)(2,1)S(1)}, bf16[2,128,1024]{1,2,0:T(8,128)(2,1)S(1)}, u32[]{:S(2)}, u32[]{:S(2)}) %collective-permute-start) | collective-permute-done | bytes 524320 | tf_op jit(solution)/shard_map/while/body/eval_jaxpr/ppermute | solution.py:13
  195.3 1.9 collective-permute-start
  197.8 12.3 %collective-permute-done = bf16[2,128,1024]{1,2,0:T(8,128)(2,1)S(1)} collective-permute-done((bf16[2,128,1024]{1,2,0:T(8,128)(2,1)S(1)}, bf16[2,128,1024]{1,2,0:T(8,128)(2,1)S(1)}, u32[]{:S(2)}, u32[]{:S(2)}) %collective-permute-start) | collective-permute-done | bytes 524320 | tf_op jit(solution)/shard_map/while/body/eval_jaxpr/ppermute | solution.py:13
  214.1 13.5 %collective-permute-done = bf16[2,128,1024]{1,2,0:T(8,128)(2,1)S(1)} collective-permute-done((bf16[2,128,1024]{1,2,0:T(8,128)(2,1)S(1)}, bf16[2,128,1024]{1,2,0:T(8,128)(2,1)S(1)}, u32[]{:S(2)}, u32[]{:S(2)}) %collective-permute-start) | collective-permute-done | bytes 524320 | tf_op jit(solution)/shard_map/while/body/eval_jaxpr/ppermute | solution.py:13
  228.8 1.9 collective-permute-start
  231.4 14.6 %collective-permute-done = bf16[2,128,1024]{1,2,0:T(8,128)(2,1)S(1)} collective-permute-done((bf16[2,128,1024]{1,2,0:T(8,128)(2,1)S(1)}, bf16[2,128,1024]{1,2,0:T(8,128)(2,1)S(1)}, u32[]{:S(2)}, u32[]{:S(2)}) %collective-permute-start) | collective-permute-done | bytes 524320 | tf_op jit(solution)/shard_map/while/body/eval_jaxpr/ppermute | solution.py:13
  249.9 15.8 %collective-permute-done = bf16[2,128,1024]{1,2,0:T(8,128)(2,1)S(1)} collective-permute-done((bf16[2,128,1024]{1,2,0:T(8,128)(2,1)S(1)}, bf16[2,128,1024]{1,2,0:T(8,128)(2,1)S(1)}, u32[]{:S(2)}, u32[]{:S(2)}) %collective-permute-start) | collective-permute-done | bytes 524320 | tf_op jit(solution)/shard_map/while/body/eval_jaxpr/ppermute | solution.py:13
  269.6 16.9 %collective-permute-done = bf16[2,128,1024]{1,2,0:T(8,128)(2,1)S(1)} collective-permute-done((bf16[2,128,1024]{1,2,0:T(8,128)(2,1)S(1)}, bf16[2,128,1024]{1,2,0:T(8,128)(2,1)S(1)}, u32[]{:S(2)}, u32[]{:S(2)}) %collective-permute-start) | collective-permute-done | bytes 524320 | tf_op jit(solution)/shard_map/while/body/eval_jaxpr/ppermute | solution.py:13
  290.4 16.8 %collective-permute-done = bf16[2,128,1024]{1,2,0:T(8,128)(2,1)S(1)} collective-permute-done((bf16[2,128,1024]{1,2,0:T(8,128)(2,1)S(1)}, bf16[2,128,1024]{1,2,0:T(8,128)(2,1)S(1)}, u32[]{:S(2)}, u32[]{:S(2)}) %collective-permute-start) | collective-permute-done | bytes 524320 | tf_op jit(solution)/shard_map/while/body/eval_jaxpr/ppermute | solution.py:13
  311.1 16.0 %collective-permute-done = bf16[2,128,1024]{1,2,0:T(8,128)(2,1)S(1)} collective-permute-done((bf16[2,128,1024]{1,2,0:T(8,128)(2,1)S(1)}, bf16[2,128,1024]{1,2,0:T(8,128)(2,1)S(1)}, u32[]{:S(2)}, u32[]{:S(2)}) %collective-permute-start) | collective-permute-done | bytes 524320 | tf_op jit(solution)/shard_map/while/body/eval_jaxpr/ppermute | solution.py:13
  328.4 1.9 collective-permute-start
  330.9 15.1 %collective-permute-done = bf16[2,128,1024]{1,2,0:T(8,128)(2,1)S(1)} collective-permute-done((bf16[2,128,1024]{1,2,0:T(8,128)(2,1)S(1)}, bf16[2,128,1024]{1,2,0:T(8,128)(2,1)S(1)}, u32[]{:S(2)}, u32[]{:S(2)}) %collective-permute-start) | collective-permute-done | bytes 524320 | tf_op jit(solution)/shard_map/while/body/eval_jaxpr/ppermute | solution.py:13
  349.9 14.3 %collective-permute-done = bf16[2,128,1024]{1,2,0:T(8,128)(2,1)S(1)} collective-permute-done((bf16[2,128,1024]{1,2,0:T(8,128)(2,1)S(1)}, bf16[2,128,1024]{1,2,0:T(8,128)(2,1)S(1)}, u32[]{:S(2)}, u32[]{:S(2)}) %collective-permute-start) | collective-permute-done | bytes 524320 | tf_op jit(solution)/shard_map/while/body/eval_jaxpr/ppermute | solution.py:13
  368.1 13.4 %collective-permute-done = bf16[2,128,1024]{1,2,0:T(8,128)(2,1)S(1)} collective-permute-done((bf16[2,128,1024]{1,2,0:T(8,128)(2,1)S(1)}, bf16[2,128,1024]{1,2,0:T(8,128)(2,1)S(1)}, u32[]{:S(2)}, u32[]{:S(2)}) %collective-permute-start) | collective-permute-done | bytes 524320 | tf_op jit(solution)/shard_map/while/body/eval_jaxpr/ppermute | solution.py:13
  385.4 12.5 %collective-permute-done = bf16[2,128,1024]{1,2,0:T(8,128)(2,1)S(1)} collective-permute-done((bf16[2,128,1024]{1,2,0:T(8,128)(2,1)S(1)}, bf16[2,128,1024]{1,2,0:T(8,128)(2,1)S(1)}, u32[]{:S(2)}, u32[]{:S(2)}) %collective-permute-start) | collective-permute-done | bytes 524320 | tf_op jit(solution)/shard_map/while/body/eval_jaxpr/ppermute | solution.py:13
  401.8 11.8 %collective-permute-done = bf16[2,128,1024]{1,2,0:T(8,128)(2,1)S(1)} collective-permute-done((bf16[2,128,1024]{1,2,0:T(8,128)(2,1)S(1)}, bf16[2,128,1024]{1,2,0:T(8,128)(2,1)S(1)}, u32[]{:S(2)}, u32[]{:S(2)}) %collective-permute-start) | collective-permute-done | bytes 524320 | tf_op jit(solution)/shard_map/while/body/eval_jaxpr/ppermute | solution.py:13
  417.5 11.8 %collective-permute-done = bf16[2,128,1024]{1,2,0:T(8,128)(2,1)S(1)} collective-permute-done((bf16[2,128,1024]{1,2,0:T(8,128)(2,1)S(1)}, bf16[2,128,1024]{1,2,0:T(8,128)(2,1)S(1)}, u32[]{:S(2)}, u32[]{:S(2)}) %collective-permute-start) | collective-permute-done | bytes 524320 | tf_op jit(solution)/shard_map/while/body/eval_jaxpr/ppermute | solution.py:13
  433.2 11.8 %collective-permute-done = bf16[2,128,1024]{1,2,0:T(8,128)(2,1)S(1)} collective-permute-done((bf16[2,128,1024]{1,2,0:T(8,128)(2,1)S(1)}, bf16[2,128,1024]{1,2,0:T(8,128)(2,1)S(1)}, u32[]{:S(2)}, u32[]{:S(2)}) %collective-permute-start) | collective-permute-done | bytes 524320 | tf_op jit(solution)/shard_map/while/body/eval_jaxpr/ppermute | solution.py:13
  449.0 12.1 %collective-permute-done = bf16[2,128,1024]{1,2,0:T(8,128)(2,1)S(1)} collective-permute-done((bf16[2,128,1024]{1,2,0:T(8,128)(2,1)S(1)}, bf16[2,128,1024]{1,2,0:T(8,128)(2,1)S(1)}, u32[]{:S(2)}, u32[]{:S(2)}) %collective-permute-start) | collective-permute-done | bytes 524320 | tf_op jit(solution)/shard_map/while/body/eval_jaxpr/ppermute | solution.py:13
  464.9 13.2 %collective-permute-done = bf16[2,128,1024]{1,2,0:T(8,128)(2,1)S(1)} collective-permute-done((bf16[2,128,1024]{1,2,0:T(8,128)(2,1)S(1)}, bf16[2,128,1024]{1,2,0:T(8,128)(2,1)S(1)}, u32[]{:S(2)}, u32[]{:S(2)}) %collective-permute-start) | collective-permute-done | bytes 524320 | tf_op jit(solution)/shard_map/while/body/eval_jaxpr/ppermute | solution.py:13
  482.1 14.4 %collective-permute-done = bf16[2,128,1024]{1,2,0:T(8,128)(2,1)S(1)} collective-permute-done((bf16[2,128,1024]{1,2,0:T(8,128)(2,1)S(1)}, bf16[2,128,1024]{1,2,0:T(8,128)(2,1)S(1)}, u32[]{:S(2)}, u32[]{:S(2)}) %collective-permute-start) | collective-permute-done | bytes 524320 | tf_op jit(solution)/shard_map/while/body/eval_jaxpr/ppermute | solution.py:13
  500.4 15.5 %collective-permute-done = bf16[2,128,1024]{1,2,0:T(8,128)(2,1)S(1)} collective-permute-done((bf16[2,128,1024]{1,2,0:T(8,128)(2,1)S(1)}, bf16[2,128,1024]{1,2,0:T(8,128)(2,1)S(1)}, u32[]{:S(2)}, u32[]{:S(2)}) %collective-permute-start) | collective-permute-done | bytes 524320 | tf_op jit(solution)/shard_map/while/body/eval_jaxpr/ppermute | solution.py:13
  519.8 16.7 %collective-permute-done = bf16[2,128,1024]{1,2,0:T(8,128)(2,1)S(1)} collective-permute-done((bf16[2,128,1024]{1,2,0:T(8,128)(2,1)S(1)}, bf16[2,128,1024]{1,2,0:T(8,128)(2,1)S(1)}, u32[]{:S(2)}, u32[]{:S(2)}) %collective-permute-start) | collective-permute-done | bytes 524320 | tf_op jit(solution)/shard_map/while/body/eval_jaxpr/ppermute | solution.py:13
  540.4 17.0 %collective-permute-done = bf16[2,128,1024]{1,2,0:T(8,128)(2,1)S(1)} collective-permute-done((bf16[2,128,1024]{1,2,0:T(8,128)(2,1)S(1)}, bf16[2,128,1024]{1,2,0:T(8,128)(2,1)S(1)}, u32[]{:S(2)}, u32[]{:S(2)}) %collective-permute-start) | collective-permute-done | bytes 524320 | tf_op jit(solution)/shard_map/while/body/eval_jaxpr/ppermute | solution.py:13
  561.3 16.2 %collective-permute-done = bf16[2,128,1024]{1,2,0:T(8,128)(2,1)S(1)} collective-permute-done((bf16[2,128,1024]{1,2,0:T(8,128)(2,1)S(1)}, bf16[2,128,1024]{1,2,0:T(8,128)(2,1)S(1)}, u32[]{:S(2)}, u32[]{:S(2)}) %collective-permute-start) | collective-permute-done | bytes 524320 | tf_op jit(solution)/shard_map/while/body/eval_jaxpr/ppermute | solution.py:13
  581.4 14.5 %collective-permute-done = bf16[2,128,1024]{1,2,0:T(8,128)(2,1)S(1)} collective-permute-done((bf16[2,128,1024]{1,2,0:T(8,128)(2,1)S(1)}, bf16[2,128,1024]{1,2,0:T(8,128)(2,1)S(1)}, u32[]{:S(2)}, u32[]{:S(2)}) %collective-permute-start) | collective-permute-done | bytes 524320 | tf_op jit(solution)/shard_map/while/body/eval_jaxpr/ppermute | solution.py:13
  599.7 11.8 %collective-permute-done = bf16[2,128,1024]{1,2,0:T(8,128)(2,1)S(1)} collective-permute-done((bf16[2,128,1024]{1,2,0:T(8,128)(2,1)S(1)}, bf16[2,128,1024]{1,2,0:T(8,128)(2,1)S(1)}, u32[]{:S(2)}, u32[]{:S(2)}) %collective-permute-start) | collective-permute-done | bytes 524320 | tf_op jit(solution)/shard_map/while/body/eval_jaxpr/ppermute | solution.py:13
  613.6 18.1 %all_to_all.10 = bf16[4,32,1024]{2,0,1:T(4,128)(2,1)S(1)} all-to-all(bf16[4,32,1024]{2,0,1:T(4,128)(2,1)S(1)} %copy.55), channel_id=1, replica_groups=mesh['dp'=16,'ctx'=32] {'ctx'}, dimensions={1} | all-to-all | bytes 524288 | tf_op jit(solution)/shard_map/all_to_all | solution.py:128
  (465 shorter events, 132.2 us)
Async XLA Ops:
  1.8 45.5 %collective-permute-start.1 = (bf16[127,1024]{1,0:T(8,128)(2,1)S(1)}, bf16[127,1024]{1,0:T(8,128)(2,1)S(1)}, u32[]{:S(2)}, u32[]{:S(2)}) collective-permute-start(bf16[127,1024]{1,0:T(8,128)(2,1)S(1)} %slice.26), channel_id=1, source_target_pairs={{0,1},{1,2},{2,3},{3,4},{4,5},{5,6},{6,7},{7,8},{8,9},{9,10},{10,1... | collective-permute-start | bytes 780296 | tf_op jit(solution)/shard_map/ppermute | solution.py:19
  7.1 49.2 %all-to-all-start = ((bf16[4,32,1024]{2,0,1:T(4,128)(2,1)}), bf16[4,32,1024]{2,0,1:T(4,128)(2,1)S(1)}, u32[]{:S(2)}, u32[]{:S(2)}) async-start(bf16[4,32,1024]{2,0,1:T(4,128)(2,1)} %copy.49), calls=%async_computation | async-start | bytes 524288 | tf_op jit(solution)/shard_map/all_to_all | solution.py:116
  45.9 8.2 %copy-start = (bf16[128,1024]{1,0:T(8,128)(2,1)S(1)}, bf16[128,1024]{1,0:T(8,128)(2,1)}, u32[]{:S(2)}) copy-start(bf16[128,1024]{1,0:T(8,128)(2,1)} %param.14) | copy-start | bytes 786436
  45.9 8.2 %copy-start.2 = (f32[1024]{0:T(1024)S(1)}, f32[1024]{0:T(1024)}, u32[]{:S(2)}) copy-start(f32[1024]{0:T(1024)} %param.17) | copy-start | bytes 12292
  45.9 9.0 %copy-start.1 = (bf16[128,1024]{1,0:T(8,128)(2,1)S(1)}, bf16[128,1024]{1,0:T(8,128)(2,1)}, u32[]{:S(2)}) copy-start(bf16[128,1024]{1,0:T(8,128)(2,1)} %param.19) | copy-start | bytes 786436
  58.6 18.3 %collective-permute-start = (bf16[2,128,1024]{1,2,0:T(8,128)(2,1)S(1)}, bf16[2,128,1024]{1,2,0:T(8,128)(2,1)S(1)}, u32[]{:S(2)}, u32[]{:S(2)}) collective-permute-start(bf16[2,128,1024]{1,2,0:T(8,128)(2,1)S(1)} %get-tuple-element.522), channel_id=1, source_target_pairs={{0,1},{1,2},{2,3},{3,4},{4,5},{5,6},{6,7},{7,8},{8,9},{9,10},{10,1... | collective-permute-start | bytes 1572872 | tf_op jit(solution)/shard_map/while/body/eval_jaxpr/ppermute | solution.py:13
  78.2 17.4 %collective-permute-start = (bf16[2,128,1024]{1,2,0:T(8,128)(2,1)S(1)}, bf16[2,128,1024]{1,2,0:T(8,128)(2,1)S(1)}, u32[]{:S(2)}, u32[]{:S(2)}) collective-permute-start(bf16[2,128,1024]{1,2,0:T(8,128)(2,1)S(1)} %get-tuple-element.522), channel_id=1, source_target_pairs={{0,1},{1,2},{2,3},{3,4},{4,5},{5,6},{6,7},{7,8},{8,9},{9,10},{10,1... | collective-permute-start | bytes 1572872 | tf_op jit(solution)/shard_map/while/body/eval_jaxpr/ppermute | solution.py:13
  97.0 16.6 %collective-permute-start = (bf16[2,128,1024]{1,2,0:T(8,128)(2,1)S(1)}, bf16[2,128,1024]{1,2,0:T(8,128)(2,1)S(1)}, u32[]{:S(2)}, u32[]{:S(2)}) collective-permute-start(bf16[2,128,1024]{1,2,0:T(8,128)(2,1)S(1)} %get-tuple-element.522), channel_id=1, source_target_pairs={{0,1},{1,2},{2,3},{3,4},{4,5},{5,6},{6,7},{7,8},{8,9},{9,10},{10,1... | collective-permute-start | bytes 1572872 | tf_op jit(solution)/shard_map/while/body/eval_jaxpr/ppermute | solution.py:13
  114.9 15.7 %collective-permute-start = (bf16[2,128,1024]{1,2,0:T(8,128)(2,1)S(1)}, bf16[2,128,1024]{1,2,0:T(8,128)(2,1)S(1)}, u32[]{:S(2)}, u32[]{:S(2)}) collective-permute-start(bf16[2,128,1024]{1,2,0:T(8,128)(2,1)S(1)} %get-tuple-element.522), channel_id=1, source_target_pairs={{0,1},{1,2},{2,3},{3,4},{4,5},{5,6},{6,7},{7,8},{8,9},{9,10},{10,1... | collective-permute-start | bytes 1572872 | tf_op jit(solution)/shard_map/while/body/eval_jaxpr/ppermute | solution.py:13
  131.9 14.9 %collective-permute-start = (bf16[2,128,1024]{1,2,0:T(8,128)(2,1)S(1)}, bf16[2,128,1024]{1,2,0:T(8,128)(2,1)S(1)}, u32[]{:S(2)}, u32[]{:S(2)}) collective-permute-start(bf16[2,128,1024]{1,2,0:T(8,128)(2,1)S(1)} %get-tuple-element.522), channel_id=1, source_target_pairs={{0,1},{1,2},{2,3},{3,4},{4,5},{5,6},{6,7},{7,8},{8,9},{9,10},{10,1... | collective-permute-start | bytes 1572872 | tf_op jit(solution)/shard_map/while/body/eval_jaxpr/ppermute | solution.py:13
  148.1 14.4 %collective-permute-start = (bf16[2,128,1024]{1,2,0:T(8,128)(2,1)S(1)}, bf16[2,128,1024]{1,2,0:T(8,128)(2,1)S(1)}, u32[]{:S(2)}, u32[]{:S(2)}) collective-permute-start(bf16[2,128,1024]{1,2,0:T(8,128)(2,1)S(1)} %get-tuple-element.522), channel_id=1, source_target_pairs={{0,1},{1,2},{2,3},{3,4},{4,5},{5,6},{6,7},{7,8},{8,9},{9,10},{10,1... | collective-permute-start | bytes 1572872 | tf_op jit(solution)/shard_map/while/body/eval_jaxpr/ppermute | solution.py:13
  163.8 14.4 %collective-permute-start = (bf16[2,128,1024]{1,2,0:T(8,128)(2,1)S(1)}, bf16[2,128,1024]{1,2,0:T(8,128)(2,1)S(1)}, u32[]{:S(2)}, u32[]{:S(2)}) collective-permute-start(bf16[2,128,1024]{1,2,0:T(8,128)(2,1)S(1)} %get-tuple-element.522), channel_id=1, source_target_pairs={{0,1},{1,2},{2,3},{3,4},{4,5},{5,6},{6,7},{7,8},{8,9},{9,10},{10,1... | collective-permute-start | bytes 1572872 | tf_op jit(solution)/shard_map/while/body/eval_jaxpr/ppermute | solution.py:13
  179.6 14.4 %collective-permute-start = (bf16[2,128,1024]{1,2,0:T(8,128)(2,1)S(1)}, bf16[2,128,1024]{1,2,0:T(8,128)(2,1)S(1)}, u32[]{:S(2)}, u32[]{:S(2)}) collective-permute-start(bf16[2,128,1024]{1,2,0:T(8,128)(2,1)S(1)} %get-tuple-element.522), channel_id=1, source_target_pairs={{0,1},{1,2},{2,3},{3,4},{4,5},{5,6},{6,7},{7,8},{8,9},{9,10},{10,1... | collective-permute-start | bytes 1572872 | tf_op jit(solution)/shard_map/while/body/eval_jaxpr/ppermute | solution.py:13
  195.3 14.9 %collective-permute-start = (bf16[2,128,1024]{1,2,0:T(8,128)(2,1)S(1)}, bf16[2,128,1024]{1,2,0:T(8,128)(2,1)S(1)}, u32[]{:S(2)}, u32[]{:S(2)}) collective-permute-start(bf16[2,128,1024]{1,2,0:T(8,128)(2,1)S(1)} %get-tuple-element.522), channel_id=1, source_target_pairs={{0,1},{1,2},{2,3},{3,4},{4,5},{5,6},{6,7},{7,8},{8,9},{9,10},{10,1... | collective-permute-start | bytes 1572872 | tf_op jit(solution)/shard_map/while/body/eval_jaxpr/ppermute | solution.py:13
  211.5 16.0 %collective-permute-start = (bf16[2,128,1024]{1,2,0:T(8,128)(2,1)S(1)}, bf16[2,128,1024]{1,2,0:T(8,128)(2,1)S(1)}, u32[]{:S(2)}, u32[]{:S(2)}) collective-permute-start(bf16[2,128,1024]{1,2,0:T(8,128)(2,1)S(1)} %get-tuple-element.522), channel_id=1, source_target_pairs={{0,1},{1,2},{2,3},{3,4},{4,5},{5,6},{6,7},{7,8},{8,9},{9,10},{10,1... | collective-permute-start | bytes 1572872 | tf_op jit(solution)/shard_map/while/body/eval_jaxpr/ppermute | solution.py:13
  228.8 17.2 %collective-permute-start = (bf16[2,128,1024]{1,2,0:T(8,128)(2,1)S(1)}, bf16[2,128,1024]{1,2,0:T(8,128)(2,1)S(1)}, u32[]{:S(2)}, u32[]{:S(2)}) collective-permute-start(bf16[2,128,1024]{1,2,0:T(8,128)(2,1)S(1)} %get-tuple-element.522), channel_id=1, source_target_pairs={{0,1},{1,2},{2,3},{3,4},{4,5},{5,6},{6,7},{7,8},{8,9},{9,10},{10,1... | collective-permute-start | bytes 1572872 | tf_op jit(solution)/shard_map/while/body/eval_jaxpr/ppermute | solution.py:13
  247.3 18.3 %collective-permute-start = (bf16[2,128,1024]{1,2,0:T(8,128)(2,1)S(1)}, bf16[2,128,1024]{1,2,0:T(8,128)(2,1)S(1)}, u32[]{:S(2)}, u32[]{:S(2)}) collective-permute-start(bf16[2,128,1024]{1,2,0:T(8,128)(2,1)S(1)} %get-tuple-element.522), channel_id=1, source_target_pairs={{0,1},{1,2},{2,3},{3,4},{4,5},{5,6},{6,7},{7,8},{8,9},{9,10},{10,1... | collective-permute-start | bytes 1572872 | tf_op jit(solution)/shard_map/while/body/eval_jaxpr/ppermute | solution.py:13
  267.0 19.5 %collective-permute-start = (bf16[2,128,1024]{1,2,0:T(8,128)(2,1)S(1)}, bf16[2,128,1024]{1,2,0:T(8,128)(2,1)S(1)}, u32[]{:S(2)}, u32[]{:S(2)}) collective-permute-start(bf16[2,128,1024]{1,2,0:T(8,128)(2,1)S(1)} %get-tuple-element.522), channel_id=1, source_target_pairs={{0,1},{1,2},{2,3},{3,4},{4,5},{5,6},{6,7},{7,8},{8,9},{9,10},{10,1... | collective-permute-start | bytes 1572872 | tf_op jit(solution)/shard_map/while/body/eval_jaxpr/ppermute | solution.py:13
  287.8 19.4 %collective-permute-start = (bf16[2,128,1024]{1,2,0:T(8,128)(2,1)S(1)}, bf16[2,128,1024]{1,2,0:T(8,128)(2,1)S(1)}, u32[]{:S(2)}, u32[]{:S(2)}) collective-permute-start(bf16[2,128,1024]{1,2,0:T(8,128)(2,1)S(1)} %get-tuple-element.522), channel_id=1, source_target_pairs={{0,1},{1,2},{2,3},{3,4},{4,5},{5,6},{6,7},{7,8},{8,9},{9,10},{10,1... | collective-permute-start | bytes 1572872 | tf_op jit(solution)/shard_map/while/body/eval_jaxpr/ppermute | solution.py:13
  308.5 18.5 %collective-permute-start = (bf16[2,128,1024]{1,2,0:T(8,128)(2,1)S(1)}, bf16[2,128,1024]{1,2,0:T(8,128)(2,1)S(1)}, u32[]{:S(2)}, u32[]{:S(2)}) collective-permute-start(bf16[2,128,1024]{1,2,0:T(8,128)(2,1)S(1)} %get-tuple-element.522), channel_id=1, source_target_pairs={{0,1},{1,2},{2,3},{3,4},{4,5},{5,6},{6,7},{7,8},{8,9},{9,10},{10,1... | collective-permute-start | bytes 1572872 | tf_op jit(solution)/shard_map/while/body/eval_jaxpr/ppermute | solution.py:13
  328.4 17.7 %collective-permute-start = (bf16[2,128,1024]{1,2,0:T(8,128)(2,1)S(1)}, bf16[2,128,1024]{1,2,0:T(8,128)(2,1)S(1)}, u32[]{:S(2)}, u32[]{:S(2)}) collective-permute-start(bf16[2,128,1024]{1,2,0:T(8,128)(2,1)S(1)} %get-tuple-element.522), channel_id=1, source_target_pairs={{0,1},{1,2},{2,3},{3,4},{4,5},{5,6},{6,7},{7,8},{8,9},{9,10},{10,1... | collective-permute-start | bytes 1572872 | tf_op jit(solution)/shard_map/while/body/eval_jaxpr/ppermute | solution.py:13
  347.4 16.8 %collective-permute-start = (bf16[2,128,1024]{1,2,0:T(8,128)(2,1)S(1)}, bf16[2,128,1024]{1,2,0:T(8,128)(2,1)S(1)}, u32[]{:S(2)}, u32[]{:S(2)}) collective-permute-start(bf16[2,128,1024]{1,2,0:T(8,128)(2,1)S(1)} %get-tuple-element.522), channel_id=1, source_target_pairs={{0,1},{1,2},{2,3},{3,4},{4,5},{5,6},{6,7},{7,8},{8,9},{9,10},{10,1... | collective-permute-start | bytes 1572872 | tf_op jit(solution)/shard_map/while/body/eval_jaxpr/ppermute | solution.py:13
  365.5 16.0 %collective-permute-start = (bf16[2,128,1024]{1,2,0:T(8,128)(2,1)S(1)}, bf16[2,128,1024]{1,2,0:T(8,128)(2,1)S(1)}, u32[]{:S(2)}, u32[]{:S(2)}) collective-permute-start(bf16[2,128,1024]{1,2,0:T(8,128)(2,1)S(1)} %get-tuple-element.522), channel_id=1, source_target_pairs={{0,1},{1,2},{2,3},{3,4},{4,5},{5,6},{6,7},{7,8},{8,9},{9,10},{10,1... | collective-permute-start | bytes 1572872 | tf_op jit(solution)/shard_map/while/body/eval_jaxpr/ppermute | solution.py:13
  382.8 15.1 %collective-permute-start = (bf16[2,128,1024]{1,2,0:T(8,128)(2,1)S(1)}, bf16[2,128,1024]{1,2,0:T(8,128)(2,1)S(1)}, u32[]{:S(2)}, u32[]{:S(2)}) collective-permute-start(bf16[2,128,1024]{1,2,0:T(8,128)(2,1)S(1)} %get-tuple-element.522), channel_id=1, source_target_pairs={{0,1},{1,2},{2,3},{3,4},{4,5},{5,6},{6,7},{7,8},{8,9},{9,10},{10,1... | collective-permute-start | bytes 1572872 | tf_op jit(solution)/shard_map/while/body/eval_jaxpr/ppermute | solution.py:13
  399.2 14.4 %collective-permute-start = (bf16[2,128,1024]{1,2,0:T(8,128)(2,1)S(1)}, bf16[2,128,1024]{1,2,0:T(8,128)(2,1)S(1)}, u32[]{:S(2)}, u32[]{:S(2)}) collective-permute-start(bf16[2,128,1024]{1,2,0:T(8,128)(2,1)S(1)} %get-tuple-element.522), channel_id=1, source_target_pairs={{0,1},{1,2},{2,3},{3,4},{4,5},{5,6},{6,7},{7,8},{8,9},{9,10},{10,1... | collective-permute-start | bytes 1572872 | tf_op jit(solution)/shard_map/while/body/eval_jaxpr/ppermute | solution.py:13
  415.0 14.4 %collective-permute-start = (bf16[2,128,1024]{1,2,0:T(8,128)(2,1)S(1)}, bf16[2,128,1024]{1,2,0:T(8,128)(2,1)S(1)}, u32[]{:S(2)}, u32[]{:S(2)}) collective-permute-start(bf16[2,128,1024]{1,2,0:T(8,128)(2,1)S(1)} %get-tuple-element.522), channel_id=1, source_target_pairs={{0,1},{1,2},{2,3},{3,4},{4,5},{5,6},{6,7},{7,8},{8,9},{9,10},{10,1... | collective-permute-start | bytes 1572872 | tf_op jit(solution)/shard_map/while/body/eval_jaxpr/ppermute | solution.py:13
  430.7 14.4 %collective-permute-start = (bf16[2,128,1024]{1,2,0:T(8,128)(2,1)S(1)}, bf16[2,128,1024]{1,2,0:T(8,128)(2,1)S(1)}, u32[]{:S(2)}, u32[]{:S(2)}) collective-permute-start(bf16[2,128,1024]{1,2,0:T(8,128)(2,1)S(1)} %get-tuple-element.522), channel_id=1, source_target_pairs={{0,1},{1,2},{2,3},{3,4},{4,5},{5,6},{6,7},{7,8},{8,9},{9,10},{10,1... | collective-permute-start | bytes 1572872 | tf_op jit(solution)/shard_map/while/body/eval_jaxpr/ppermute | solution.py:13
  446.4 14.7 %collective-permute-start = (bf16[2,128,1024]{1,2,0:T(8,128)(2,1)S(1)}, bf16[2,128,1024]{1,2,0:T(8,128)(2,1)S(1)}, u32[]{:S(2)}, u32[]{:S(2)}) collective-permute-start(bf16[2,128,1024]{1,2,0:T(8,128)(2,1)S(1)} %get-tuple-element.522), channel_id=1, source_target_pairs={{0,1},{1,2},{2,3},{3,4},{4,5},{5,6},{6,7},{7,8},{8,9},{9,10},{10,1... | collective-permute-start | bytes 1572872 | tf_op jit(solution)/shard_map/while/body/eval_jaxpr/ppermute | solution.py:13
  462.4 15.8 %collective-permute-start = (bf16[2,128,1024]{1,2,0:T(8,128)(2,1)S(1)}, bf16[2,128,1024]{1,2,0:T(8,128)(2,1)S(1)}, u32[]{:S(2)}, u32[]{:S(2)}) collective-permute-start(bf16[2,128,1024]{1,2,0:T(8,128)(2,1)S(1)} %get-tuple-element.522), channel_id=1, source_target_pairs={{0,1},{1,2},{2,3},{3,4},{4,5},{5,6},{6,7},{7,8},{8,9},{9,10},{10,1... | collective-permute-start | bytes 1572872 | tf_op jit(solution)/shard_map/while/body/eval_jaxpr/ppermute | solution.py:13
  479.5 17.0 %collective-permute-start = (bf16[2,128,1024]{1,2,0:T(8,128)(2,1)S(1)}, bf16[2,128,1024]{1,2,0:T(8,128)(2,1)S(1)}, u32[]{:S(2)}, u32[]{:S(2)}) collective-permute-start(bf16[2,128,1024]{1,2,0:T(8,128)(2,1)S(1)} %get-tuple-element.522), channel_id=1, source_target_pairs={{0,1},{1,2},{2,3},{3,4},{4,5},{5,6},{6,7},{7,8},{8,9},{9,10},{10,1... | collective-permute-start | bytes 1572872 | tf_op jit(solution)/shard_map/while/body/eval_jaxpr/ppermute | solution.py:13
  497.8 18.1 %collective-permute-start = (bf16[2,128,1024]{1,2,0:T(8,128)(2,1)S(1)}, bf16[2,128,1024]{1,2,0:T(8,128)(2,1)S(1)}, u32[]{:S(2)}, u32[]{:S(2)}) collective-permute-start(bf16[2,128,1024]{1,2,0:T(8,128)(2,1)S(1)} %get-tuple-element.522), channel_id=1, source_target_pairs={{0,1},{1,2},{2,3},{3,4},{4,5},{5,6},{6,7},{7,8},{8,9},{9,10},{10,1... | collective-permute-start | bytes 1572872 | tf_op jit(solution)/shard_map/while/body/eval_jaxpr/ppermute | solution.py:13
  517.2 19.3 %collective-permute-start = (bf16[2,128,1024]{1,2,0:T(8,128)(2,1)S(1)}, bf16[2,128,1024]{1,2,0:T(8,128)(2,1)S(1)}, u32[]{:S(2)}, u32[]{:S(2)}) collective-permute-start(bf16[2,128,1024]{1,2,0:T(8,128)(2,1)S(1)} %get-tuple-element.522), channel_id=1, source_target_pairs={{0,1},{1,2},{2,3},{3,4},{4,5},{5,6},{6,7},{7,8},{8,9},{9,10},{10,1... | collective-permute-start | bytes 1572872 | tf_op jit(solution)/shard_map/while/body/eval_jaxpr/ppermute | solution.py:13
  537.8 19.6 %collective-permute-start = (bf16[2,128,1024]{1,2,0:T(8,128)(2,1)S(1)}, bf16[2,128,1024]{1,2,0:T(8,128)(2,1)S(1)}, u32[]{:S(2)}, u32[]{:S(2)}) collective-permute-start(bf16[2,128,1024]{1,2,0:T(8,128)(2,1)S(1)} %get-tuple-element.522), channel_id=1, source_target_pairs={{0,1},{1,2},{2,3},{3,4},{4,5},{5,6},{6,7},{7,8},{8,9},{9,10},{10,1... | collective-permute-start | bytes 1572872 | tf_op jit(solution)/shard_map/while/body/eval_jaxpr/ppermute | solution.py:13
  558.7 18.8 %collective-permute-start = (bf16[2,128,1024]{1,2,0:T(8,128)(2,1)S(1)}, bf16[2,128,1024]{1,2,0:T(8,128)(2,1)S(1)}, u32[]{:S(2)}, u32[]{:S(2)}) collective-permute-start(bf16[2,128,1024]{1,2,0:T(8,128)(2,1)S(1)} %get-tuple-element.522), channel_id=1, source_target_pairs={{0,1},{1,2},{2,3},{3,4},{4,5},{5,6},{6,7},{7,8},{8,9},{9,10},{10,1... | collective-permute-start | bytes 1572872 | tf_op jit(solution)/shard_map/while/body/eval_jaxpr/ppermute | solution.py:13
  578.8 17.0 %collective-permute-start = (bf16[2,128,1024]{1,2,0:T(8,128)(2,1)S(1)}, bf16[2,128,1024]{1,2,0:T(8,128)(2,1)S(1)}, u32[]{:S(2)}, u32[]{:S(2)}) collective-permute-start(bf16[2,128,1024]{1,2,0:T(8,128)(2,1)S(1)} %get-tuple-element.522), channel_id=1, source_target_pairs={{0,1},{1,2},{2,3},{3,4},{4,5},{5,6},{6,7},{7,8},{8,9},{9,10},{10,1... | collective-permute-start | bytes 1572872 | tf_op jit(solution)/shard_map/while/body/eval_jaxpr/ppermute | solution.py:13
  597.1 14.4 %collective-permute-start = (bf16[2,128,1024]{1,2,0:T(8,128)(2,1)S(1)}, bf16[2,128,1024]{1,2,0:T(8,128)(2,1)S(1)}, u32[]{:S(2)}, u32[]{:S(2)}) collective-permute-start(bf16[2,128,1024]{1,2,0:T(8,128)(2,1)S(1)} %get-tuple-element.522), channel_id=1, source_target_pairs={{0,1},{1,2},{2,3},{3,4},{4,5},{5,6},{6,7},{7,8},{8,9},{9,10},{10,1... | collective-permute-start | bytes 1572872 | tf_op jit(solution)/shard_map/while/body/eval_jaxpr/ppermute | solution.py:13
where the time goes:
time: 634 us; the launch traced here: 632 us
  waiting for transfers between devices  432 us (68%)
  starting transfers between devices  77.6 us (12%)
  local copies, waits for them, and re-layouts  35 us (6%)
  matrix products  32.3 us (5%)
  loops' own time  23.1 us (4%)
  blocking collectives  18.1 us (3%)
  other arithmetic  13 us (2%)
    ppermute x31, waiting for transfers between devices, passed_along(): lax.ppermute(array, axis, [(i, (i + by) % devices) for i in range(devices)])  432 us
    ppermute x31, starting transfers between devices, passed_along(): lax.ppermute(array, axis, [(i, (i + by) % devices) for i in range(devices)])  61.3 us
    another operation x1, loops' own time, attend(): lax.fori_loop(0, members - 1, chain_step, (first_state, stacked))  21.4 us
    all_to_all x1, blocking collectives, shards(): lax.all_to_all(attended.reshape(per_source, members, channels), 'ctx', sp...  18.1 us
    reshape x1, local copies, waits for them, and re-layouts, shards(): jnp.tile(padded, (1, TAPS))[:, :TAPS * window_rows]  15.9 us
    dot_general x32, matrix products, update_block(): jnp.einsum('thp,phd->thd', weights.astype(jnp.bfloat16), value_heads, pre...  15 us
    all_to_all x1, starting transfers between devices, shards(): lax.all_to_all(query_rows.reshape(per_source, members, channels), 'ctx',...  12.9 us
  transfers between devices with their start and end apart: 33, of which 31 were waited for; matrix products, arithmetic and copies ran while one was open for 6% of the time, Pallas kernels for 0%

commit v1 on v0

--- a/solution.py
+++ b/solution.py
@@ -125,12 +125,18 @@
     query_pos = (source * local_rows + offset * members + my_index).reshape(local_rows)
     local_queries = spread.reshape(local_rows, channels)
     attended = attend(local_queries, query_pos, key_rows, hyena_out)
-    returned = lax.all_to_all(
-        attended.reshape(per_source, members, channels),
-        "ctx",
-        split_axis=1,
-        concat_axis=1,
-        tiled=True,
+    returned = jnp.concatenate(
+        lax.all_to_all(
+            jnp.stack(
+                jnp.split(
+                    attended.reshape(per_source, members, channels), lax.axis_size("ctx"), axis=1
+                )
+            ),
+            "ctx",
+            0,
+            0,
+        ),
+        axis=1,
     )
     attended = returned.reshape(local_rows, channels)
     return (hyena_out, attended)

time: 634 us -> 634 us (level)
  no operation moved by 1% of the time
where the time goes in v1:
time: 634 us; the launch traced here: 632 us
  waiting for transfers between devices  432 us (68%)
  starting transfers between devices  77.6 us (12%)
  local copies, waits for them, and re-layouts  38 us (6%)
  matrix products  31.4 us (5%)
  loops' own time  23.3 us (4%)
  blocking collectives  18.1 us (3%)
  other arithmetic  10.6 us (2%)
    ppermute x31, waiting for transfers between devices, passed_along(): lax.ppermute(array, axis, [(i, (i + by) % devices) for i in range(devices)])  432 us
    ppermute x31, starting transfers between devices, passed_along(): lax.ppermute(array, axis, [(i, (i + by) % devices) for i in range(devices)])  61.3 us
    another operation x1, loops' own time, attend(): lax.fori_loop(0, members - 1, chain_step, (first_state, stacked))  21.7 us
    all_to_all x1, blocking collectives, shards(): lax.all_to_all(jnp.stack(jnp.split(attended.reshape(per_source, members,...  18.1 us
    reshape x1, local copies, waits for them, and re-layouts, shards(): jnp.tile(padded, (1, TAPS))[:, :TAPS * window_rows]  16 us
    dot_general x32, matrix products, update_block(): jnp.einsum('thp,phd->thd', weights.astype(jnp.bfloat16), value_heads, pre...  14.1 us
    all_to_all x1, starting transfers between devices, shards(): lax.all_to_all(query_rows.reshape(per_source, members, channels), 'ctx',...  12.9 us
  transfers between devices with their start and end apart: 33, of which 31 were waited for; matrix products, arithmetic and copies ran while one was open for 6% of the time, Pallas kernels for 0%

profile of v1, /device:TPU:56, one launch (start us, length us, event | category | flops | bytes accessed | tf_op | source)
XLA Modules:
  0.0 632.3 jit_solution(8170904308298449261)
XLA Ops:
  3.1 3.4 collective-permute-start.1
  8.4 12.9 %all-to-all-start = ((bf16[4,32,1024]{2,0,1:T(4,128)(2,1)}), bf16[4,32,1024]{2,0,1:T(4,128)(2,1)S(1)}, u32[]{:S(2)}, u32[]{:S(2)}) async-start(bf16[4,32,1024]{2,0,1:T(4,128)(2,1)} %copy.926), calls=%async_computation | async-start | bytes 524288 | tf_op jit(solution)/shard_map/all_to_all | solution.py:116
  22.8 4.7 copy.975
  27.5 3.7 slice.27
  31.3 16.0 %reshape.132 = f32[64,128,255]{2,1,0:T(8,128)} reshape(f32[64,32640]{1,0:T(8,128)} %slice.27) | data formatting | bytes 16711680 | tf_op jit(solution)/shard_map/reshape | solution.py:103
  49.1 6.3 fusion.34
  57.5 554.2 %while.22 = (s32[]{:T(128)}, f32[128,8]{0,1:T(8,128)S(1)}, f32[128,8]{0,1:T(8,128)S(1)}, f32[128,8,128]{2,0,1:T(8,128)S(1)}, bf16[2,128,1024]{1,2,0:T(8,128)(2,1...) while((s32[]{:T(128)}, f32[128,8]{0,1:T(8,128)S(1)}, ...), condition=%wide.region_10.11_spmd.clone, body=%wide.region_5.10_spmd.clone.sunk | while | flops 68569488 | bytes 7736928 | solution.py:86
  57.6 3.7 collective-permute-start
  61.9 14.0 %collective-permute-done = bf16[2,128,1024]{1,2,0:T(8,128)(2,1)S(1)} collective-permute-done((bf16[2,128,1024]{1,2,0:T(8,128)(2,1)S(1)}, bf16[2,128,1024]{1,2,0:T(8,128)(2,1)S(1)}, u32[]{:S(2)}, u32[]{:S(2)}) %collective-permute-start) | collective-permute-done | bytes 524320 | tf_op jit(solution)/shard_map/while/body/eval_jaxpr/ppermute | solution.py:13
  79.8 14.9 %collective-permute-done = bf16[2,128,1024]{1,2,0:T(8,128)(2,1)S(1)} collective-permute-done((bf16[2,128,1024]{1,2,0:T(8,128)(2,1)S(1)}, bf16[2,128,1024]{1,2,0:T(8,128)(2,1)S(1)}, u32[]{:S(2)}, u32[]{:S(2)}) %collective-permute-start) | collective-permute-done | bytes 524320 | tf_op jit(solution)/shard_map/while/body/eval_jaxpr/ppermute | solution.py:13
  96.0 1.9 collective-permute-start
  98.6 14.0 %collective-permute-done = bf16[2,128,1024]{1,2,0:T(8,128)(2,1)S(1)} collective-permute-done((bf16[2,128,1024]{1,2,0:T(8,128)(2,1)S(1)}, bf16[2,128,1024]{1,2,0:T(8,128)(2,1)S(1)}, u32[]{:S(2)}, u32[]{:S(2)}) %collective-permute-start) | collective-permute-done | bytes 524320 | tf_op jit(solution)/shard_map/while/body/eval_jaxpr/ppermute | solution.py:13
  116.5 13.2 %collective-permute-done = bf16[2,128,1024]{1,2,0:T(8,128)(2,1)S(1)} collective-permute-done((bf16[2,128,1024]{1,2,0:T(8,128)(2,1)S(1)}, bf16[2,128,1024]{1,2,0:T(8,128)(2,1)S(1)}, u32[]{:S(2)}, u32[]{:S(2)}) %collective-permute-start) | collective-permute-done | bytes 524320 | tf_op jit(solution)/shard_map/while/body/eval_jaxpr/ppermute | solution.py:13
  133.5 12.3 %collective-permute-done = bf16[2,128,1024]{1,2,0:T(8,128)(2,1)S(1)} collective-permute-done((bf16[2,128,1024]{1,2,0:T(8,128)(2,1)S(1)}, bf16[2,128,1024]{1,2,0:T(8,128)(2,1)S(1)}, u32[]{:S(2)}, u32[]{:S(2)}) %collective-permute-start) | collective-permute-done | bytes 524320 | tf_op jit(solution)/shard_map/while/body/eval_jaxpr/ppermute | solution.py:13
  149.7 11.8 %collective-permute-done = bf16[2,128,1024]{1,2,0:T(8,128)(2,1)S(1)} collective-permute-done((bf16[2,128,1024]{1,2,0:T(8,128)(2,1)S(1)}, bf16[2,128,1024]{1,2,0:T(8,128)(2,1)S(1)}, u32[]{:S(2)}, u32[]{:S(2)}) %collective-permute-start) | collective-permute-done | bytes 524320 | tf_op jit(solution)/shard_map/while/body/eval_jaxpr/ppermute | solution.py:13
  165.5 11.8 %collective-permute-done = bf16[2,128,1024]{1,2,0:T(8,128)(2,1)S(1)} collective-permute-done((bf16[2,128,1024]{1,2,0:T(8,128)(2,1)S(1)}, bf16[2,128,1024]{1,2,0:T(8,128)(2,1)S(1)}, u32[]{:S(2)}, u32[]{:S(2)}) %collective-permute-start) | collective-permute-done | bytes 524320 | tf_op jit(solution)/shard_map/while/body/eval_jaxpr/ppermute | solution.py:13
  178.6 1.9 collective-permute-start
  181.2 11.8 %collective-permute-done = bf16[2,128,1024]{1,2,0:T(8,128)(2,1)S(1)} collective-permute-done((bf16[2,128,1024]{1,2,0:T(8,128)(2,1)S(1)}, bf16[2,128,1024]{1,2,0:T(8,128)(2,1)S(1)}, u32[]{:S(2)}, u32[]{:S(2)}) %collective-permute-start) | collective-permute-done | bytes 524320 | tf_op jit(solution)/shard_map/while/body/eval_jaxpr/ppermute | solution.py:13
  194.3 1.9 collective-permute-start
  196.9 12.3 %collective-permute-done = bf16[2,128,1024]{1,2,0:T(8,128)(2,1)S(1)} collective-permute-done((bf16[2,128,1024]{1,2,0:T(8,128)(2,1)S(1)}, bf16[2,128,1024]{1,2,0:T(8,128)(2,1)S(1)}, u32[]{:S(2)}, u32[]{:S(2)}) %collective-permute-start) | collective-permute-done | bytes 524320 | tf_op jit(solution)/shard_map/while/body/eval_jaxpr/ppermute | solution.py:13
  210.5 1.9 collective-permute-start
  213.1 13.5 %collective-permute-done = bf16[2,128,1024]{1,2,0:T(8,128)(2,1)S(1)} collective-permute-done((bf16[2,128,1024]{1,2,0:T(8,128)(2,1)S(1)}, bf16[2,128,1024]{1,2,0:T(8,128)(2,1)S(1)}, u32[]{:S(2)}, u32[]{:S(2)}) %collective-permute-start) | collective-permute-done | bytes 524320 | tf_op jit(solution)/shard_map/while/body/eval_jaxpr/ppermute | solution.py:13
  227.9 1.9 collective-permute-start
  230.4 14.6 %collective-permute-done = bf16[2,128,1024]{1,2,0:T(8,128)(2,1)S(1)} collective-permute-done((bf16[2,128,1024]{1,2,0:T(8,128)(2,1)S(1)}, bf16[2,128,1024]{1,2,0:T(8,128)(2,1)S(1)}, u32[]{:S(2)}, u32[]{:S(2)}) %collective-permute-start) | collective-permute-done | bytes 524320 | tf_op jit(solution)/shard_map/while/body/eval_jaxpr/ppermute | solution.py:13
  249.0 15.8 %collective-permute-done = bf16[2,128,1024]{1,2,0:T(8,128)(2,1)S(1)} collective-permute-done((bf16[2,128,1024]{1,2,0:T(8,128)(2,1)S(1)}, bf16[2,128,1024]{1,2,0:T(8,128)(2,1)S(1)}, u32[]{:S(2)}, u32[]{:S(2)}) %collective-permute-start) | collective-permute-done | bytes 524320 | tf_op jit(solution)/shard_map/while/body/eval_jaxpr/ppermute | solution.py:13
  268.6 16.9 %collective-permute-done = bf16[2,128,1024]{1,2,0:T(8,128)(2,1)S(1)} collective-permute-done((bf16[2,128,1024]{1,2,0:T(8,128)(2,1)S(1)}, bf16[2,128,1024]{1,2,0:T(8,128)(2,1)S(1)}, u32[]{:S(2)}, u32[]{:S(2)}) %collective-permute-start) | collective-permute-done | bytes 524320 | tf_op jit(solution)/shard_map/while/body/eval_jaxpr/ppermute | solution.py:13
  289.4 16.8 %collective-permute-done = bf16[2,128,1024]{1,2,0:T(8,128)(2,1)S(1)} collective-permute-done((bf16[2,128,1024]{1,2,0:T(8,128)(2,1)S(1)}, bf16[2,128,1024]{1,2,0:T(8,128)(2,1)S(1)}, u32[]{:S(2)}, u32[]{:S(2)}) %collective-permute-start) | collective-permute-done | bytes 524320 | tf_op jit(solution)/shard_map/while/body/eval_jaxpr/ppermute | solution.py:13
  310.1 16.0 %collective-permute-done = bf16[2,128,1024]{1,2,0:T(8,128)(2,1)S(1)} collective-permute-done((bf16[2,128,1024]{1,2,0:T(8,128)(2,1)S(1)}, bf16[2,128,1024]{1,2,0:T(8,128)(2,1)S(1)}, u32[]{:S(2)}, u32[]{:S(2)}) %collective-permute-start) | collective-permute-done | bytes 524320 | tf_op jit(solution)/shard_map/while/body/eval_jaxpr/ppermute | solution.py:13
  327.4 1.9 collective-permute-start
  330.0 15.1 %collective-permute-done = bf16[2,128,1024]{1,2,0:T(8,128)(2,1)S(1)} collective-permute-done((bf16[2,128,1024]{1,2,0:T(8,128)(2,1)S(1)}, bf16[2,128,1024]{1,2,0:T(8,128)(2,1)S(1)}, u32[]{:S(2)}, u32[]{:S(2)}) %collective-permute-start) | collective-permute-done | bytes 524320 | tf_op jit(solution)/shard_map/while/body/eval_jaxpr/ppermute | solution.py:13
  346.4 1.9 collective-permute-start
  349.0 14.3 %collective-permute-done = bf16[2,128,1024]{1,2,0:T(8,128)(2,1)S(1)} collective-permute-done((bf16[2,128,1024]{1,2,0:T(8,128)(2,1)S(1)}, bf16[2,128,1024]{1,2,0:T(8,128)(2,1)S(1)}, u32[]{:S(2)}, u32[]{:S(2)}) %collective-permute-start) | collective-permute-done | bytes 524320 | tf_op jit(solution)/shard_map/while/body/eval_jaxpr/ppermute | solution.py:13
  367.1 13.4 %collective-permute-done = bf16[2,128,1024]{1,2,0:T(8,128)(2,1)S(1)} collective-permute-done((bf16[2,128,1024]{1,2,0:T(8,128)(2,1)S(1)}, bf16[2,128,1024]{1,2,0:T(8,128)(2,1)S(1)}, u32[]{:S(2)}, u32[]{:S(2)}) %collective-permute-start) | collective-permute-done | bytes 524320 | tf_op jit(solution)/shard_map/while/body/eval_jaxpr/ppermute | solution.py:13
  384.4 12.5 %collective-permute-done = bf16[2,128,1024]{1,2,0:T(8,128)(2,1)S(1)} collective-permute-done((bf16[2,128,1024]{1,2,0:T(8,128)(2,1)S(1)}, bf16[2,128,1024]{1,2,0:T(8,128)(2,1)S(1)}, u32[]{:S(2)}, u32[]{:S(2)}) %collective-permute-start) | collective-permute-done | bytes 524320 | tf_op jit(solution)/shard_map/while/body/eval_jaxpr/ppermute | solution.py:13
  400.9 11.8 %collective-permute-done = bf16[2,128,1024]{1,2,0:T(8,128)(2,1)S(1)} collective-permute-done((bf16[2,128,1024]{1,2,0:T(8,128)(2,1)S(1)}, bf16[2,128,1024]{1,2,0:T(8,128)(2,1)S(1)}, u32[]{:S(2)}, u32[]{:S(2)}) %collective-permute-start) | collective-permute-done | bytes 524320 | tf_op jit(solution)/shard_map/while/body/eval_jaxpr/ppermute | solution.py:13
  416.6 11.8 %collective-permute-done = bf16[2,128,1024]{1,2,0:T(8,128)(2,1)S(1)} collective-permute-done((bf16[2,128,1024]{1,2,0:T(8,128)(2,1)S(1)}, bf16[2,128,1024]{1,2,0:T(8,128)(2,1)S(1)}, u32[]{:S(2)}, u32[]{:S(2)}) %collective-permute-start) | collective-permute-done | bytes 524320 | tf_op jit(solution)/shard_map/while/body/eval_jaxpr/ppermute | solution.py:13
  429.7 1.9 collective-permute-start
  432.3 11.8 %collective-permute-done = bf16[2,128,1024]{1,2,0:T(8,128)(2,1)S(1)} collective-permute-done((bf16[2,128,1024]{1,2,0:T(8,128)(2,1)S(1)}, bf16[2,128,1024]{1,2,0:T(8,128)(2,1)S(1)}, u32[]{:S(2)}, u32[]{:S(2)}) %collective-permute-start) | collective-permute-done | bytes 524320 | tf_op jit(solution)/shard_map/while/body/eval_jaxpr/ppermute | solution.py:13
  448.0 12.1 %collective-permute-done = bf16[2,128,1024]{1,2,0:T(8,128)(2,1)S(1)} collective-permute-done((bf16[2,128,1024]{1,2,0:T(8,128)(2,1)S(1)}, bf16[2,128,1024]{1,2,0:T(8,128)(2,1)S(1)}, u32[]{:S(2)}, u32[]{:S(2)}) %collective-permute-start) | collective-permute-done | bytes 524320 | tf_op jit(solution)/shard_map/while/body/eval_jaxpr/ppermute | solution.py:13
  464.0 13.2 %collective-permute-done = bf16[2,128,1024]{1,2,0:T(8,128)(2,1)S(1)} collective-permute-done((bf16[2,128,1024]{1,2,0:T(8,128)(2,1)S(1)}, bf16[2,128,1024]{1,2,0:T(8,128)(2,1)S(1)}, u32[]{:S(2)}, u32[]{:S(2)}) %collective-permute-start) | collective-permute-done | bytes 524320 | tf_op jit(solution)/shard_map/while/body/eval_jaxpr/ppermute | solution.py:13
  481.1 14.4 %collective-permute-done = bf16[2,128,1024]{1,2,0:T(8,128)(2,1)S(1)} collective-permute-done((bf16[2,128,1024]{1,2,0:T(8,128)(2,1)S(1)}, bf16[2,128,1024]{1,2,0:T(8,128)(2,1)S(1)}, u32[]{:S(2)}, u32[]{:S(2)}) %collective-permute-start) | collective-permute-done | bytes 524320 | tf_op jit(solution)/shard_map/while/body/eval_jaxpr/ppermute | solution.py:13
  499.4 15.5 %collective-permute-done = bf16[2,128,1024]{1,2,0:T(8,128)(2,1)S(1)} collective-permute-done((bf16[2,128,1024]{1,2,0:T(8,128)(2,1)S(1)}, bf16[2,128,1024]{1,2,0:T(8,128)(2,1)S(1)}, u32[]{:S(2)}, u32[]{:S(2)}) %collective-permute-start) | collective-permute-done | bytes 524320 | tf_op jit(solution)/shard_map/while/body/eval_jaxpr/ppermute | solution.py:13
  518.8 16.7 %collective-permute-done = bf16[2,128,1024]{1,2,0:T(8,128)(2,1)S(1)} collective-permute-done((bf16[2,128,1024]{1,2,0:T(8,128)(2,1)S(1)}, bf16[2,128,1024]{1,2,0:T(8,128)(2,1)S(1)}, u32[]{:S(2)}, u32[]{:S(2)}) %collective-permute-start) | collective-permute-done | bytes 524320 | tf_op jit(solution)/shard_map/while/body/eval_jaxpr/ppermute | solution.py:13
  539.4 17.0 %collective-permute-done = bf16[2,128,1024]{1,2,0:T(8,128)(2,1)S(1)} collective-permute-done((bf16[2,128,1024]{1,2,0:T(8,128)(2,1)S(1)}, bf16[2,128,1024]{1,2,0:T(8,128)(2,1)S(1)}, u32[]{:S(2)}, u32[]{:S(2)}) %collective-permute-start) | collective-permute-done | bytes 524320 | tf_op jit(solution)/shard_map/while/body/eval_jaxpr/ppermute | solution.py:13
  560.3 16.2 %collective-permute-done = bf16[2,128,1024]{1,2,0:T(8,128)(2,1)S(1)} collective-permute-done((bf16[2,128,1024]{1,2,0:T(8,128)(2,1)S(1)}, bf16[2,128,1024]{1,2,0:T(8,128)(2,1)S(1)}, u32[]{:S(2)}, u32[]{:S(2)}) %collective-permute-start) | collective-permute-done | bytes 524320 | tf_op jit(solution)/shard_map/while/body/eval_jaxpr/ppermute | solution.py:13
  580.4 14.4 %collective-permute-done = bf16[2,128,1024]{1,2,0:T(8,128)(2,1)S(1)} collective-permute-done((bf16[2,128,1024]{1,2,0:T(8,128)(2,1)S(1)}, bf16[2,128,1024]{1,2,0:T(8,128)(2,1)S(1)}, u32[]{:S(2)}, u32[]{:S(2)}) %collective-permute-start) | collective-permute-done | bytes 524320 | tf_op jit(solution)/shard_map/while/body/eval_jaxpr/ppermute | solution.py:13
  598.7 11.8 %collective-permute-done = bf16[2,128,1024]{1,2,0:T(8,128)(2,1)S(1)} collective-permute-done((bf16[2,128,1024]{1,2,0:T(8,128)(2,1)S(1)}, bf16[2,128,1024]{1,2,0:T(8,128)(2,1)S(1)}, u32[]{:S(2)}, u32[]{:S(2)}) %collective-permute-start) | collective-permute-done | bytes 524320 | tf_op jit(solution)/shard_map/while/body/eval_jaxpr/ppermute | solution.py:13
  613.4 18.1 %all_to_all.10 = bf16[32,4,1,1024]{3,1,2,0:T(4,128)(2,1)S(1)} all-to-all(bf16[32,4,1,1024]{3,1,2,0:T(4,128)(2,1)S(1)} %constant_dynamic-update-slice_fusion), channel_id=1, replica_groups=mesh['dp'=16,'ctx'=32] {'ctx'}, dimensions={0} | all-to-all | bytes 524288 | tf_op jit(solution)/shard_map/all_to_all | solution.py:129
  (502 shorter events, 131.1 us)
Async XLA Ops:
  3.1 45.7 %collective-permute-start.1 = (bf16[127,1024]{0,1:T(8,128)(2,1)S(1)}, bf16[127,1024]{0,1:T(8,128)(2,1)S(1)}, u32[]{:S(2)}, u32[]{:S(2)}) collective-permute-start(bf16[127,1024]{0,1:T(8,128)(2,1)S(1)} %slice.26), channel_id=1, source_target_pairs={{0,1},{1,2},{2,3},{3,4},{4,5},{5,6},{6,7},{7,8},{8,9},{9,10},{10,1... | collective-permute-start | bytes 780296 | tf_op jit(solution)/shard_map/ppermute | solution.py:19
  8.4 47.8 %all-to-all-start = ((bf16[4,32,1024]{2,0,1:T(4,128)(2,1)}), bf16[4,32,1024]{2,0,1:T(4,128)(2,1)S(1)}, u32[]{:S(2)}, u32[]{:S(2)}) async-start(bf16[4,32,1024]{2,0,1:T(4,128)(2,1)} %copy.926), calls=%async_computation | async-start | bytes 524288 | tf_op jit(solution)/shard_map/all_to_all | solution.py:116
  31.3 16.0 %copy-start.1 = (bf16[128,1024]{1,0:T(8,128)(2,1)S(1)}, bf16[128,1024]{1,0:T(8,128)(2,1)}, u32[]{:S(2)}) copy-start(bf16[128,1024]{1,0:T(8,128)(2,1)} %param.14) | copy-start | bytes 786436
  47.3 8.1 %copy-start.3 = (f32[1024]{0:T(1024)S(1)}, f32[1024]{0:T(1024)}, u32[]{:S(2)}) copy-start(f32[1024]{0:T(1024)} %param.17) | copy-start | bytes 12292
  47.3 8.5 %copy-start.2 = (bf16[128,1024]{1,0:T(8,128)(2,1)S(1)}, bf16[128,1024]{1,0:T(8,128)(2,1)}, u32[]{:S(2)}) copy-start(bf16[128,1024]{1,0:T(8,128)(2,1)} %param.19) | copy-start | bytes 786436
  55.8 1.8 copy-start
  57.6 18.3 %collective-permute-start = (bf16[2,128,1024]{1,2,0:T(8,128)(2,1)S(1)}, bf16[2,128,1024]{1,2,0:T(8,128)(2,1)S(1)}, u32[]{:S(2)}, u32[]{:S(2)}) collective-permute-start(bf16[2,128,1024]{1,2,0:T(8,128)(2,1)S(1)} %get-tuple-element.1022), channel_id=1, source_target_pairs={{0,1},{1,2},{2,3},{3,4},{4,5},{5,6},{6,7},{7,8},{8,9},{9,10},{10,1... | collective-permute-start | bytes 1572872 | tf_op jit(solution)/shard_map/while/body/eval_jaxpr/ppermute | solution.py:13
  77.2 17.5 %collective-permute-start = (bf16[2,128,1024]{1,2,0:T(8,128)(2,1)S(1)}, bf16[2,128,1024]{1,2,0:T(8,128)(2,1)S(1)}, u32[]{:S(2)}, u32[]{:S(2)}) collective-permute-start(bf16[2,128,1024]{1,2,0:T(8,128)(2,1)S(1)} %get-tuple-element.1022), channel_id=1, source_target_pairs={{0,1},{1,2},{2,3},{3,4},{4,5},{5,6},{6,7},{7,8},{8,9},{9,10},{10,1... | collective-permute-start | bytes 1572872 | tf_op jit(solution)/shard_map/while/body/eval_jaxpr/ppermute | solution.py:13
  96.0 16.6 %collective-permute-start = (bf16[2,128,1024]{1,2,0:T(8,128)(2,1)S(1)}, bf16[2,128,1024]{1,2,0:T(8,128)(2,1)S(1)}, u32[]{:S(2)}, u32[]{:S(2)}) collective-permute-start(bf16[2,128,1024]{1,2,0:T(8,128)(2,1)S(1)} %get-tuple-element.1022), channel_id=1, source_target_pairs={{0,1},{1,2},{2,3},{3,4},{4,5},{5,6},{6,7},{7,8},{8,9},{9,10},{10,1... | collective-permute-start | bytes 1572872 | tf_op jit(solution)/shard_map/while/body/eval_jaxpr/ppermute | solution.py:13
  113.9 15.7 %collective-permute-start = (bf16[2,128,1024]{1,2,0:T(8,128)(2,1)S(1)}, bf16[2,128,1024]{1,2,0:T(8,128)(2,1)S(1)}, u32[]{:S(2)}, u32[]{:S(2)}) collective-permute-start(bf16[2,128,1024]{1,2,0:T(8,128)(2,1)S(1)} %get-tuple-element.1022), channel_id=1, source_target_pairs={{0,1},{1,2},{2,3},{3,4},{4,5},{5,6},{6,7},{7,8},{8,9},{9,10},{10,1... | collective-permute-start | bytes 1572872 | tf_op jit(solution)/shard_map/while/body/eval_jaxpr/ppermute | solution.py:13
  131.0 14.9 %collective-permute-start = (bf16[2,128,1024]{1,2,0:T(8,128)(2,1)S(1)}, bf16[2,128,1024]{1,2,0:T(8,128)(2,1)S(1)}, u32[]{:S(2)}, u32[]{:S(2)}) collective-permute-start(bf16[2,128,1024]{1,2,0:T(8,128)(2,1)S(1)} %get-tuple-element.1022), channel_id=1, source_target_pairs={{0,1},{1,2},{2,3},{3,4},{4,5},{5,6},{6,7},{7,8},{8,9},{9,10},{10,1... | collective-permute-start | bytes 1572872 | tf_op jit(solution)/shard_map/while/body/eval_jaxpr/ppermute | solution.py:13
  147.2 14.4 %collective-permute-start = (bf16[2,128,1024]{1,2,0:T(8,128)(2,1)S(1)}, bf16[2,128,1024]{1,2,0:T(8,128)(2,1)S(1)}, u32[]{:S(2)}, u32[]{:S(2)}) collective-permute-start(bf16[2,128,1024]{1,2,0:T(8,128)(2,1)S(1)} %get-tuple-element.1022), channel_id=1, source_target_pairs={{0,1},{1,2},{2,3},{3,4},{4,5},{5,6},{6,7},{7,8},{8,9},{9,10},{10,1... | collective-permute-start | bytes 1572872 | tf_op jit(solution)/shard_map/while/body/eval_jaxpr/ppermute | solution.py:13
  162.9 14.4 %collective-permute-start = (bf16[2,128,1024]{1,2,0:T(8,128)(2,1)S(1)}, bf16[2,128,1024]{1,2,0:T(8,128)(2,1)S(1)}, u32[]{:S(2)}, u32[]{:S(2)}) collective-permute-start(bf16[2,128,1024]{1,2,0:T(8,128)(2,1)S(1)} %get-tuple-element.1022), channel_id=1, source_target_pairs={{0,1},{1,2},{2,3},{3,4},{4,5},{5,6},{6,7},{7,8},{8,9},{9,10},{10,1... | collective-permute-start | bytes 1572872 | tf_op jit(solution)/shard_map/while/body/eval_jaxpr/ppermute | solution.py:13
  178.6 14.4 %collective-permute-start = (bf16[2,128,1024]{1,2,0:T(8,128)(2,1)S(1)}, bf16[2,128,1024]{1,2,0:T(8,128)(2,1)S(1)}, u32[]{:S(2)}, u32[]{:S(2)}) collective-permute-start(bf16[2,128,1024]{1,2,0:T(8,128)(2,1)S(1)} %get-tuple-element.1022), channel_id=1, source_target_pairs={{0,1},{1,2},{2,3},{3,4},{4,5},{5,6},{6,7},{7,8},{8,9},{9,10},{10,1... | collective-permute-start | bytes 1572872 | tf_op jit(solution)/shard_map/while/body/eval_jaxpr/ppermute | solution.py:13
  194.3 14.9 %collective-permute-start = (bf16[2,128,1024]{1,2,0:T(8,128)(2,1)S(1)}, bf16[2,128,1024]{1,2,0:T(8,128)(2,1)S(1)}, u32[]{:S(2)}, u32[]{:S(2)}) collective-permute-start(bf16[2,128,1024]{1,2,0:T(8,128)(2,1)S(1)} %get-tuple-element.1022), channel_id=1, source_target_pairs={{0,1},{1,2},{2,3},{3,4},{4,5},{5,6},{6,7},{7,8},{8,9},{9,10},{10,1... | collective-permute-start | bytes 1572872 | tf_op jit(solution)/shard_map/while/body/eval_jaxpr/ppermute | solution.py:13
  210.5 16.0 %collective-permute-start = (bf16[2,128,1024]{1,2,0:T(8,128)(2,1)S(1)}, bf16[2,128,1024]{1,2,0:T(8,128)(2,1)S(1)}, u32[]{:S(2)}, u32[]{:S(2)}) collective-permute-start(bf16[2,128,1024]{1,2,0:T(8,128)(2,1)S(1)} %get-tuple-element.1022), channel_id=1, source_target_pairs={{0,1},{1,2},{2,3},{3,4},{4,5},{5,6},{6,7},{7,8},{8,9},{9,10},{10,1... | collective-permute-start | bytes 1572872 | tf_op jit(solution)/shard_map/while/body/eval_jaxpr/ppermute | solution.py:13
  227.9 17.2 %collective-permute-start = (bf16[2,128,1024]{1,2,0:T(8,128)(2,1)S(1)}, bf16[2,128,1024]{1,2,0:T(8,128)(2,1)S(1)}, u32[]{:S(2)}, u32[]{:S(2)}) collective-permute-start(bf16[2,128,1024]{1,2,0:T(8,128)(2,1)S(1)} %get-tuple-element.1022), channel_id=1, source_target_pairs={{0,1},{1,2},{2,3},{3,4},{4,5},{5,6},{6,7},{7,8},{8,9},{9,10},{10,1... | collective-permute-start | bytes 1572872 | tf_op jit(solution)/shard_map/while/body/eval_jaxpr/ppermute | solution.py:13
  246.4 18.3 %collective-permute-start = (bf16[2,128,1024]{1,2,0:T(8,128)(2,1)S(1)}, bf16[2,128,1024]{1,2,0:T(8,128)(2,1)S(1)}, u32[]{:S(2)}, u32[]{:S(2)}) collective-permute-start(bf16[2,128,1024]{1,2,0:T(8,128)(2,1)S(1)} %get-tuple-element.1022), channel_id=1, source_target_pairs={{0,1},{1,2},{2,3},{3,4},{4,5},{5,6},{6,7},{7,8},{8,9},{9,10},{10,1... | collective-permute-start | bytes 1572872 | tf_op jit(solution)/shard_map/while/body/eval_jaxpr/ppermute | solution.py:13
  266.0 19.5 %collective-permute-start = (bf16[2,128,1024]{1,2,0:T(8,128)(2,1)S(1)}, bf16[2,128,1024]{1,2,0:T(8,128)(2,1)S(1)}, u32[]{:S(2)}, u32[]{:S(2)}) collective-permute-start(bf16[2,128,1024]{1,2,0:T(8,128)(2,1)S(1)} %get-tuple-element.1022), channel_id=1, source_target_pairs={{0,1},{1,2},{2,3},{3,4},{4,5},{5,6},{6,7},{7,8},{8,9},{9,10},{10,1... | collective-permute-start | bytes 1572872 | tf_op jit(solution)/shard_map/while/body/eval_jaxpr/ppermute | solution.py:13
  286.8 19.4 %collective-permute-start = (bf16[2,128,1024]{1,2,0:T(8,128)(2,1)S(1)}, bf16[2,128,1024]{1,2,0:T(8,128)(2,1)S(1)}, u32[]{:S(2)}, u32[]{:S(2)}) collective-permute-start(bf16[2,128,1024]{1,2,0:T(8,128)(2,1)S(1)} %get-tuple-element.1022), channel_id=1, source_target_pairs={{0,1},{1,2},{2,3},{3,4},{4,5},{5,6},{6,7},{7,8},{8,9},{9,10},{10,1... | collective-permute-start | bytes 1572872 | tf_op jit(solution)/shard_map/while/body/eval_jaxpr/ppermute | solution.py:13
  307.5 18.5 %collective-permute-start = (bf16[2,128,1024]{1,2,0:T(8,128)(2,1)S(1)}, bf16[2,128,1024]{1,2,0:T(8,128)(2,1)S(1)}, u32[]{:S(2)}, u32[]{:S(2)}) collective-permute-start(bf16[2,128,1024]{1,2,0:T(8,128)(2,1)S(1)} %get-tuple-element.1022), channel_id=1, source_target_pairs={{0,1},{1,2},{2,3},{3,4},{4,5},{5,6},{6,7},{7,8},{8,9},{9,10},{10,1... | collective-permute-start | bytes 1572872 | tf_op jit(solution)/shard_map/while/body/eval_jaxpr/ppermute | solution.py:13
  327.4 17.7 %collective-permute-start = (bf16[2,128,1024]{1,2,0:T(8,128)(2,1)S(1)}, bf16[2,128,1024]{1,2,0:T(8,128)(2,1)S(1)}, u32[]{:S(2)}, u32[]{:S(2)}) collective-permute-start(bf16[2,128,1024]{1,2,0:T(8,128)(2,1)S(1)} %get-tuple-element.1022), channel_id=1, source_target_pairs={{0,1},{1,2},{2,3},{3,4},{4,5},{5,6},{6,7},{7,8},{8,9},{9,10},{10,1... | collective-permute-start | bytes 1572872 | tf_op jit(solution)/shard_map/while/body/eval_jaxpr/ppermute | solution.py:13
  346.4 16.8 %collective-permute-start = (bf16[2,128,1024]{1,2,0:T(8,128)(2,1)S(1)}, bf16[2,128,1024]{1,2,0:T(8,128)(2,1)S(1)}, u32[]{:S(2)}, u32[]{:S(2)}) collective-permute-start(bf16[2,128,1024]{1,2,0:T(8,128)(2,1)S(1)} %get-tuple-element.1022), channel_id=1, source_target_pairs={{0,1},{1,2},{2,3},{3,4},{4,5},{5,6},{6,7},{7,8},{8,9},{9,10},{10,1... | collective-permute-start | bytes 1572872 | tf_op jit(solution)/shard_map/while/body/eval_jaxpr/ppermute | solution.py:13
  364.5 16.0 %collective-permute-start = (bf16[2,128,1024]{1,2,0:T(8,128)(2,1)S(1)}, bf16[2,128,1024]{1,2,0:T(8,128)(2,1)S(1)}, u32[]{:S(2)}, u32[]{:S(2)}) collective-permute-start(bf16[2,128,1024]{1,2,0:T(8,128)(2,1)S(1)} %get-tuple-element.1022), channel_id=1, source_target_pairs={{0,1},{1,2},{2,3},{3,4},{4,5},{5,6},{6,7},{7,8},{8,9},{9,10},{10,1... | collective-permute-start | bytes 1572872 | tf_op jit(solution)/shard_map/while/body/eval_jaxpr/ppermute | solution.py:13
  381.8 15.1 %collective-permute-start = (bf16[2,128,1024]{1,2,0:T(8,128)(2,1)S(1)}, bf16[2,128,1024]{1,2,0:T(8,128)(2,1)S(1)}, u32[]{:S(2)}, u32[]{:S(2)}) collective-permute-start(bf16[2,128,1024]{1,2,0:T(8,128)(2,1)S(1)} %get-tuple-element.1022), channel_id=1, source_target_pairs={{0,1},{1,2},{2,3},{3,4},{4,5},{5,6},{6,7},{7,8},{8,9},{9,10},{10,1... | collective-permute-start | bytes 1572872 | tf_op jit(solution)/shard_map/while/body/eval_jaxpr/ppermute | solution.py:13
  398.3 14.4 %collective-permute-start = (bf16[2,128,1024]{1,2,0:T(8,128)(2,1)S(1)}, bf16[2,128,1024]{1,2,0:T(8,128)(2,1)S(1)}, u32[]{:S(2)}, u32[]{:S(2)}) collective-permute-start(bf16[2,128,1024]{1,2,0:T(8,128)(2,1)S(1)} %get-tuple-element.1022), channel_id=1, source_target_pairs={{0,1},{1,2},{2,3},{3,4},{4,5},{5,6},{6,7},{7,8},{8,9},{9,10},{10,1... | collective-permute-start | bytes 1572872 | tf_op jit(solution)/shard_map/while/body/eval_jaxpr/ppermute | solution.py:13
  414.0 14.4 %collective-permute-start = (bf16[2,128,1024]{1,2,0:T(8,128)(2,1)S(1)}, bf16[2,128,1024]{1,2,0:T(8,128)(2,1)S(1)}, u32[]{:S(2)}, u32[]{:S(2)}) collective-permute-start(bf16[2,128,1024]{1,2,0:T(8,128)(2,1)S(1)} %get-tuple-element.1022), channel_id=1, source_target_pairs={{0,1},{1,2},{2,3},{3,4},{4,5},{5,6},{6,7},{7,8},{8,9},{9,10},{10,1... | collective-permute-start | bytes 1572872 | tf_op jit(solution)/shard_map/while/body/eval_jaxpr/ppermute | solution.py:13
  429.7 14.4 %collective-permute-start = (bf16[2,128,1024]{1,2,0:T(8,128)(2,1)S(1)}, bf16[2,128,1024]{1,2,0:T(8,128)(2,1)S(1)}, u32[]{:S(2)}, u32[]{:S(2)}) collective-permute-start(bf16[2,128,1024]{1,2,0:T(8,128)(2,1)S(1)} %get-tuple-element.1022), channel_id=1, source_target_pairs={{0,1},{1,2},{2,3},{3,4},{4,5},{5,6},{6,7},{7,8},{8,9},{9,10},{10,1... | collective-permute-start | bytes 1572872 | tf_op jit(solution)/shard_map/while/body/eval_jaxpr/ppermute | solution.py:13
  445.4 14.7 %collective-permute-start = (bf16[2,128,1024]{1,2,0:T(8,128)(2,1)S(1)}, bf16[2,128,1024]{1,2,0:T(8,128)(2,1)S(1)}, u32[]{:S(2)}, u32[]{:S(2)}) collective-permute-start(bf16[2,128,1024]{1,2,0:T(8,128)(2,1)S(1)} %get-tuple-element.1022), channel_id=1, source_target_pairs={{0,1},{1,2},{2,3},{3,4},{4,5},{5,6},{6,7},{7,8},{8,9},{9,10},{10,1... | collective-permute-start | bytes 1572872 | tf_op jit(solution)/shard_map/while/body/eval_jaxpr/ppermute | solution.py:13
  461.4 15.8 %collective-permute-start = (bf16[2,128,1024]{1,2,0:T(8,128)(2,1)S(1)}, bf16[2,128,1024]{1,2,0:T(8,128)(2,1)S(1)}, u32[]{:S(2)}, u32[]{:S(2)}) collective-permute-start(bf16[2,128,1024]{1,2,0:T(8,128)(2,1)S(1)} %get-tuple-element.1022), channel_id=1, source_target_pairs={{0,1},{1,2},{2,3},{3,4},{4,5},{5,6},{6,7},{7,8},{8,9},{9,10},{10,1... | collective-permute-start | bytes 1572872 | tf_op jit(solution)/shard_map/while/body/eval_jaxpr/ppermute | solution.py:13
  478.5 17.0 %collective-permute-start = (bf16[2,128,1024]{1,2,0:T(8,128)(2,1)S(1)}, bf16[2,128,1024]{1,2,0:T(8,128)(2,1)S(1)}, u32[]{:S(2)}, u32[]{:S(2)}) collective-permute-start(bf16[2,128,1024]{1,2,0:T(8,128)(2,1)S(1)} %get-tuple-element.1022), channel_id=1, source_target_pairs={{0,1},{1,2},{2,3},{3,4},{4,5},{5,6},{6,7},{7,8},{8,9},{9,10},{10,1... | collective-permute-start | bytes 1572872 | tf_op jit(solution)/shard_map/while/body/eval_jaxpr/ppermute | solution.py:13
  496.8 18.1 %collective-permute-start = (bf16[2,128,1024]{1,2,0:T(8,128)(2,1)S(1)}, bf16[2,128,1024]{1,2,0:T(8,128)(2,1)S(1)}, u32[]{:S(2)}, u32[]{:S(2)}) collective-permute-start(bf16[2,128,1024]{1,2,0:T(8,128)(2,1)S(1)} %get-tuple-element.1022), channel_id=1, source_target_pairs={{0,1},{1,2},{2,3},{3,4},{4,5},{5,6},{6,7},{7,8},{8,9},{9,10},{10,1... | collective-permute-start | bytes 1572872 | tf_op jit(solution)/shard_map/while/body/eval_jaxpr/ppermute | solution.py:13
  516.2 19.3 %collective-permute-start = (bf16[2,128,1024]{1,2,0:T(8,128)(2,1)S(1)}, bf16[2,128,1024]{1,2,0:T(8,128)(2,1)S(1)}, u32[]{:S(2)}, u32[]{:S(2)}) collective-permute-start(bf16[2,128,1024]{1,2,0:T(8,128)(2,1)S(1)} %get-tuple-element.1022), channel_id=1, source_target_pairs={{0,1},{1,2},{2,3},{3,4},{4,5},{5,6},{6,7},{7,8},{8,9},{9,10},{10,1... | collective-permute-start | bytes 1572872 | tf_op jit(solution)/shard_map/while/body/eval_jaxpr/ppermute | solution.py:13
  536.8 19.6 %collective-permute-start = (bf16[2,128,1024]{1,2,0:T(8,128)(2,1)S(1)}, bf16[2,128,1024]{1,2,0:T(8,128)(2,1)S(1)}, u32[]{:S(2)}, u32[]{:S(2)}) collective-permute-start(bf16[2,128,1024]{1,2,0:T(8,128)(2,1)S(1)} %get-tuple-element.1022), channel_id=1, source_target_pairs={{0,1},{1,2},{2,3},{3,4},{4,5},{5,6},{6,7},{7,8},{8,9},{9,10},{10,1... | collective-permute-start | bytes 1572872 | tf_op jit(solution)/shard_map/while/body/eval_jaxpr/ppermute | solution.py:13
  557.8 18.8 %collective-permute-start = (bf16[2,128,1024]{1,2,0:T(8,128)(2,1)S(1)}, bf16[2,128,1024]{1,2,0:T(8,128)(2,1)S(1)}, u32[]{:S(2)}, u32[]{:S(2)}) collective-permute-start(bf16[2,128,1024]{1,2,0:T(8,128)(2,1)S(1)} %get-tuple-element.1022), channel_id=1, source_target_pairs={{0,1},{1,2},{2,3},{3,4},{4,5},{5,6},{6,7},{7,8},{8,9},{9,10},{10,1... | collective-permute-start | bytes 1572872 | tf_op jit(solution)/shard_map/while/body/eval_jaxpr/ppermute | solution.py:13
  577.8 16.9 %collective-permute-start = (bf16[2,128,1024]{1,2,0:T(8,128)(2,1)S(1)}, bf16[2,128,1024]{1,2,0:T(8,128)(2,1)S(1)}, u32[]{:S(2)}, u32[]{:S(2)}) collective-permute-start(bf16[2,128,1024]{1,2,0:T(8,128)(2,1)S(1)} %get-tuple-element.1022), channel_id=1, source_target_pairs={{0,1},{1,2},{2,3},{3,4},{4,5},{5,6},{6,7},{7,8},{8,9},{9,10},{10,1... | collective-permute-start | bytes 1572872 | tf_op jit(solution)/shard_map/while/body/eval_jaxpr/ppermute | solution.py:13
  596.1 14.4 %collective-permute-start = (bf16[2,128,1024]{1,2,0:T(8,128)(2,1)S(1)}, bf16[2,128,1024]{1,2,0:T(8,128)(2,1)S(1)}, u32[]{:S(2)}, u32[]{:S(2)}) collective-permute-start(bf16[2,128,1024]{1,2,0:T(8,128)(2,1)S(1)} %get-tuple-element.1022), channel_id=1, source_target_pairs={{0,1},{1,2},{2,3},{3,4},{4,5},{5,6},{6,7},{7,8},{8,9},{9,10},{10,1... | collective-permute-start | bytes 1572872 | tf_op jit(solution)/shard_map/while/body/eval_jaxpr/ppermute | solution.py:13
